TPU v7x, 512 devices: a whole 4x8x8 slice. The times are simulated.
512 devices in a mesh: req: 64 (over z, x, core), tp: 8 (over y).
Axes of the slice: x: 4, y: 8, z: 8, core: 2. Of those that a mesh axis runs over, the one named last changes fastest.
Arguments:
- queries: bfloat16 [1024, 2048], P('req', 'tp'), may hold values from -27 to 27
- fresh_cache: bfloat16 [1024, 2, 2048], P('req', None, 'tp'), may hold values from -4 to 4
- tail_cache: bfloat16 [1024, 32, 2, 2048], P('req', None, None, 'tp'), may hold values from -4 to 4
- tail_len: int32 [1024], P('req'), may hold values from 1 to 32, as said below
- pool_cache: bfloat16 [2048, 64, 2, 2048], P('req', None, None, 'tp'), may hold values from -4 to 4
- page_group: int32 [2048], P('req'), may hold values from 0 to 63, as said below
- page_start: int32 [2048], P('req'), may hold values from 0 to 16320, as said below
- prompt_len: int32 [64], replicated, may hold values from 1 to 16384, as said below
- residual: bfloat16 [1024, 2048], P('req'), may hold values from -80 to 80
- out_weight: bfloat16 [2048, 2048], P('tp'), may hold values from -0.125 to 0.125
- out_bias: bfloat16 [2048], replicated, may hold values from -0.796875 to 0.796875
- norm_gain: bfloat16 [2048], P('tp'), may hold values from 0.5 to 1.5
- norm_shift: bfloat16 [2048], P('tp'), may hold values from -0.796875 to 0.796875
Outputs:
- attention_out: bfloat16 [1024, 2048], P('req', 'tp')
- normed: bfloat16 [1024, 2048], P('req', 'tp')
Inputs may be any that keep to these rules, and one draw needn't show every extreme that they name: page_group[p] is the group whose prompt page p holds; every page holds some group's prompt; every group holds at least one page and at most 256 pages, and some group holds exactly 256; the pages of a group of n pages lie on min(n, 64) different indices of req, none holding more than ceil(n / 64) of them. The pages of a group of n pages have page_start 0, 64, ..., (n - 1) * 64, each once. `prompt_len`: a group of n pages has a prompt of (n - 1) * 64 + 1 to n * 64 positions. `tail_len`: some request has exactly 32 tail positions.
All inputs are finite; a program needn't handle non-finite values.
Results may differ from a plain program's by a relative error of at most 0.02.
Values may be sent and summed in bfloat16 or wider, within the bound.
No kernel may reach another device: no remote copies, remote signals or barrier semaphores. Data moves between devices by JAX's collectives and lax.ppermute only.
A program may use at most 64 MiB of HBM per device.

v0:
```python
import math
import jax
import jax.numpy as jnp
from jax import lax
from jax.sharding import PartitionSpec as P

HEADS = 16
HEAD = 128
PAGE = 64
masked_score = -1e30
norm_epsilon = 1e-05


def split_halves(values):
    upper_part = lax.optimization_barrier(values.astype(jnp.bfloat16))
    lower_part = (values - upper_part.astype(jnp.float32)).astype(jnp.bfloat16)
    return (upper_part, lower_part)


def local(
    queries,
    fresh_cache,
    tail_cache,
    tail_len,
    pool_cache,
    page_group,
    page_start,
    prompt_len,
    residual,
    out_weight,
    out_bias,
    norm_gain,
    norm_shift,
):
    f32 = jnp.float32
    highest = lax.Precision.HIGHEST
    row_count, feat_width = queries.shape
    heads_here = feat_width // HEAD
    inv_root = 1.0 / math.sqrt(HEAD)
    head_ids = lax.axis_index("tp") * heads_here + jnp.arange(heads_here)
    slopes = jnp.exp2(-8.0 * (head_ids.astype(f32) + 1.0) / HEADS)
    group_count = prompt_len.shape[0]
    page_count = pool_cache.shape[0]
    tail_slots = tail_cache.shape[1]
    req_index = lax.axis_index("req")
    everyone = lax.all_gather(queries, "req", axis=0, tiled=True)
    by_group = everyone.reshape(group_count, row_count, heads_here, HEAD)
    safe_group = jnp.clip(page_group, 0, group_count - 1)
    page_queries = by_group[safe_group]
    page_keys = pool_cache[:, :, 0].reshape(page_count, PAGE, heads_here, HEAD)
    page_values = pool_cache[:, :, 1].reshape(page_count, PAGE, heads_here, HEAD)
    prompt_here = prompt_len[safe_group]
    positions = page_start[:, None] + jnp.arange(PAGE)[None, :]
    usable = (positions < prompt_here[:, None]) & (page_group[:, None] >= 0)
    offsets = (positions - prompt_here[:, None]).astype(f32)
    scores = (
        jnp.einsum("pqhd,pshd->pqhs", page_queries, page_keys, preferred_element_type=f32)
        * inv_root
    )
    scores = scores + slopes[None, None, :, None] * offsets[:, None, None, :]
    scores = jnp.where(usable[:, None, None, :], scores, masked_score)
    member = page_group[:, None] == jnp.arange(group_count)[None, :]
    page_top = scores.max(-1)
    group_top = jnp.where(member[:, :, None, None], page_top[:, None], masked_score).max(0)
    group_top = group_top.reshape(group_count * row_count, heads_here)
    home_queries = queries.reshape(row_count, heads_here, HEAD)
    tail_keys = tail_cache[:, :, 0].reshape(row_count, tail_slots, heads_here, HEAD)
    tail_values = tail_cache[:, :, 1].reshape(row_count, tail_slots, heads_here, HEAD)
    fresh_keys = fresh_cache[:, 0].reshape(row_count, heads_here, HEAD)
    fresh_values = fresh_cache[:, 1].reshape(row_count, heads_here, HEAD)
    slot_ids = jnp.arange(tail_slots)
    tail_scores = (
        jnp.einsum("qhd,qjhd->qhj", home_queries, tail_keys, preferred_element_type=f32) * inv_root
    )
    tail_scores = tail_scores + slopes[None, :, None] * slot_ids.astype(f32)[None, None, :]
    tail_scores = jnp.where(
        slot_ids[None, None, :] < tail_len[:, None, None], tail_scores, masked_score
    )
    own_scores = (
        jnp.einsum("qhd,qhd->qh", home_queries, fresh_keys, preferred_element_type=f32) * inv_root
    )
    own_scores = own_scores + slopes[None, :] * tail_len.astype(f32)[:, None]
    home_top = jnp.maximum(tail_scores.max(-1), own_scores)
    mine = lax.dynamic_slice_in_dim(group_top, req_index * row_count, row_count, 0)
    merged = lax.dynamic_update_slice_in_dim(
        group_top, jnp.maximum(mine, home_top), req_index * row_count, 0
    )
    all_top = lax.pmax(merged, "req")
    reference_top = all_top.reshape(group_count, row_count, heads_here)[safe_group]
    weights = jnp.where(usable[:, None, None, :], jnp.exp(scores - reference_top[..., None]), 0.0)
    page_totals = weights.sum(-1)
    upper_part, lower_part = split_halves(weights)
    page_accum = jnp.einsum("pqhs,pshd->pqhd", upper_part, page_values, preferred_element_type=f32)
    page_accum = page_accum + jnp.einsum(
        "pqhs,pshd->pqhd", lower_part, page_values, preferred_element_type=f32
    )
    accum_upper, accum_lower = split_halves(page_accum.reshape(page_count, -1))
    spread = member.T.astype(jnp.bfloat16)
    accum = jnp.dot(spread, accum_upper, preferred_element_type=f32)
    accum = accum + jnp.dot(spread, accum_lower, preferred_element_type=f32)
    totals = jnp.dot(member.T.astype(f32), page_totals.reshape(page_count, -1), precision=highest)
    totals, accum = (
        totals.reshape(group_count * row_count, heads_here),
        accum.reshape(group_count * row_count, feat_width),
    )
    pool_totals, pool_accum = (
        lax.psum_scatter(totals, "req", scatter_dimension=0, tiled=True),
        lax.psum_scatter(accum, "req", scatter_dimension=0, tiled=True),
    )
    pool_accum = pool_accum.reshape(row_count, heads_here, HEAD)
    row_top = lax.dynamic_slice_in_dim(all_top, req_index * row_count, row_count, 0)
    tail_weights = jnp.exp(tail_scores - row_top[:, :, None])
    own_weights = jnp.exp(own_scores - row_top)
    totals = tail_weights.sum(-1) + own_weights
    upper_part, lower_part = split_halves(tail_weights)
    accum = jnp.einsum("qhj,qjhd->qhd", upper_part, tail_values, preferred_element_type=f32)
    accum = accum + jnp.einsum("qhj,qjhd->qhd", lower_part, tail_values, preferred_element_type=f32)
    home_accum = accum + own_weights[:, :, None] * fresh_values.astype(f32)
    attention = ((pool_accum + home_accum) / (pool_totals + totals)[:, :, None]).astype(
        jnp.bfloat16
    )
    attention = attention.reshape(row_count, feat_width)
    partial_value = jnp.dot(attention, out_weight, preferred_element_type=f32)
    model_width = residual.shape[1]
    own_start = lax.axis_index("tp") * feat_width
    summed = lax.psum_scatter(
        partial_value.astype(jnp.bfloat16), "tp", scatter_dimension=1, tiled=True
    ).astype(jnp.float32)
    bias_mine = lax.dynamic_slice_in_dim(out_bias, own_start, feat_width, 0).astype(f32)
    attention_mine = (summed + bias_mine[None, :]).astype(jnp.bfloat16)
    residual_mine = lax.dynamic_slice_in_dim(residual, own_start, feat_width, 1).astype(f32)
    hidden_mine = residual_mine + attention_mine.astype(f32)
    first_sum, second_sum = lax.psum(
        (jnp.sum(hidden_mine, -1), jnp.sum(hidden_mine * hidden_mine, -1)), "tp"
    )
    row_mean = (first_sum / model_width)[:, None]
    mean_square = (second_sum / model_width)[:, None]
    row_var = mean_square - row_mean * row_mean
    normed = (
        (hidden_mine - row_mean)
        * lax.rsqrt(row_var + norm_epsilon)
        * norm_gain.astype(f32)[None, :]
    )
    normed = normed + norm_shift.astype(f32)[None, :]
    return (attention_mine, normed.astype(jnp.bfloat16))


def solution(mesh):
    in_specs = (
        P("req", "tp"),
        P("req", None, "tp"),
        P("req", None, None, "tp"),
        P("req"),
        P("req", None, None, "tp"),
        P("req"),
        P("req"),
        P(),
        P("req", None),
        P("tp", None),
        P(),
        P("tp"),
        P("tp"),
    )
    out_specs = (P("req", "tp"), P("req", "tp"))
    return jax.shard_map(local, mesh=mesh, in_specs=in_specs, out_specs=out_specs, check_vma=False)
```

profile of v0, /device:TPU:2, one launch (start us, length us, event | category | flops | bytes accessed | tf_op | source)
XLA Modules:
  0.0 536.2 jit_solution(4596948644088355456)
XLA Ops:
  7.2 0.7 compare_select_fusion
  8.0 0.7 broadcast_compare_fusion
  8.6 0.7 iota_compare_fusion
  9.4 56.0 %all_gather.3 = bf16[1024,256]{1,0:T(8,128)(2,1)S(1)} all-gather(bf16[16,256]{1,0:T(8,128)(2,1)} %param.13), channel_id=1, replica_groups=mesh['req'=64,'tp'=8] {'req'}, dimensions={0}, use_global_device_ids=true | all-gather | bytes 532480 | tf_op jit(solution)/shard_map/all_gather | solution.py:46
  65.4 0.7 reshape.271
  66.1 0.7 reshape.226
  66.8 0.7 iota_compare_fusion.3
  67.5 0.7 convert_element_type.100
  68.2 1.4 gather_fusion
  69.5 0.7 subtract_convert_fusion.5
  70.3 0.7 fusion.31
  71.0 0.1 reshape.224
  71.2 0.6 gather_fusion.1
  71.8 10.7 %slice_reduce_fusion = (bf16[32,64,256]{2,1,0:T(8,128)(2,1)S(1)}, bf16[32,64,256]{2,1,0:T(8,128)(2,1)S(1)}) fusion(bf16[32,64,2,256]{3,2,1,0:T(2,128)(2,1)} %param.17), kind=kLoop, calls=%fused_computation.5 | loop fusion | bytes 4194304 | tf_op jit(solution)/shard_map/slice | solution.py:51
  82.6 0.8 fusion.48
  83.4 0.2 select_reduce_fusion
  83.7 0.1 reshape.225
  83.9 2.9 slice_reduce_fusion.2
  86.8 0.1 fusion.25
  87.0 1.2 fusion.17
  88.2 0.1 fusion.46
  88.3 0.2 dynamic_update_slice.3
  88.6 124.1 %pmax.7 = f32[1024,2]{0,1:T(2,128)S(1)} all-reduce(f32[1024,2]{0,1:T(2,128)S(1)} %dynamic_update_slice.3), channel_id=1, replica_groups=mesh['req'=64,'tp'=8] {'req'}, use_global_device_ids=true, to_apply=%region_3.4 | all-reduce | flops 2048 | bytes 16384 | tf_op jit(solution)/shard_map/pmax | solution.py:88
  212.8 0.6 gather_fusion.2
  213.4 0.4 fusion.11
  213.8 0.4 fusion.5
  214.2 0.5 fusion
  214.7 0.3 copy.55
  215.0 0.4 reshape.228
  215.5 0.4 fusion.35
  215.9 0.4 convolution_add_fusion
  216.3 1.1 reshape.229
  217.8 0.3 fusion.38
  218.1 0.3 reshape.232
  218.4 1.3 dynamic-slice
  220.3 249.1 %all-reduce = f32[1024,2]{1,0:T(8,128)S(1)} all-reduce(f32[1024,2]{1,0:T(8,128)S(1)} %reshape.232), channel_id=3, replica_groups=mesh['req'=64,'tp'=8] {'req'}, use_global_device_ids=true, to_apply=%region_6.7.clone | all-reduce | flops 2048 | bytes 16384
  469.6 0.2 fusion.36
  469.8 0.1 copy.56
  470.0 0.2 fusion.13
  470.2 0.2 fusion.15
  470.4 0.7 reshape.230
  471.1 0.1 fusion.32
  471.2 0.9 convolution_convert_fusion
  472.2 0.8 dynamic-slice_convert_fusion
  472.9 38.6 %reduce-scatter.5.cloned.1.call-done = bf16[16,256]{1,0:T(8,128)(2,1)} async-done(((bf16[16,2048]{1,0:T(8,128)(2,1)}), bf16[16,256]{1,0:T(8,128)(2,1)}) %reduce-scatter.5.cloned.1.call-update) | async-done | bytes 8208 | tf_op jit(solution)/shard_map/reduce_scatter | solution.py:126
  511.6 0.8 fusion.33
  512.4 15.6 %all-reduce.1 = (f32[16]{0:T(128)S(1)}, f32[16]{0:T(128)S(1)}) all-reduce(f32[16]{0:T(128)S(1)} %get-tuple-element.7, f32[16]{0:T(128)S(1)} %get-tuple-element.6), channel_id=1, replica_groups=mesh['req'=64,'tp'=8] {'tp'}, use_global_device_ids=true, to_apply=%region_12.13 | all-reduce | flops 32 | bytes 256 | tf_op jit(solution)/shard_map/psum | solution.py:133
  528.0 1.4 add_convert_fusion
  (43 shorter events, 1.4 us)
Async XLA Ops:
  7.2 464.0 %copy-start = (bf16[256,2048]{1,0:T(8,128)(2,1)S(1)}, bf16[256,2048]{1,0:T(8,128)(2,1)}, u32[]{:S(2)}) copy-start(bf16[256,2048]{1,0:T(8,128)(2,1)} %param.22) | copy-start | bytes 3145732
  7.2 463.2 %reduce-scatter.3.cloned.1.call-start = ((), (), s32[]{:S(2)}) async-start(), calls=%async_computation.2 | async-start | bytes 1064960 | tf_op jit(solution)/shard_map/reduce_scatter | solution.py:108
  82.5 1.3 copy-start.1
  82.5 4.2 copy-start.2
  214.7 0.8 copy-start.4
  217.5 254.6 %copy-start.5 = (bf16[256]{0:T(256)(128)(2,1)S(1)}, bf16[256]{0:T(256)(128)(2,1)}, u32[]{:S(2)}) copy-start(bf16[256]{0:T(256)(128)(2,1)} %param.24) | copy-start | bytes 1540
  217.5 254.6 %copy-start.6 = (bf16[256]{0:T(256)(128)(2,1)S(1)}, bf16[256]{0:T(256)(128)(2,1)}, u32[]{:S(2)}) copy-start(bf16[256]{0:T(256)(128)(2,1)} %param.25) | copy-start | bytes 1540
  217.5 294.0 %reduce-scatter.5.cloned.1.call-start = ((), (), s32[]{:S(2)}) async-start(), calls=%async_computation.3 | async-start | bytes 73728 | tf_op jit(solution)/shard_map/reduce_scatter | solution.py:126
  512.4 17.0 %copy-start.3 = (bf16[16,256]{1,0:T(8,128)(2,1)}, bf16[16,256]{1,0:T(8,128)(2,1)S(1)}, u32[]{:S(2)}) copy-start(bf16[16,256]{1,0:T(8,128)(2,1)S(1)} %get-tuple-element.10) | copy-start | bytes 24580
Sparse Core Ops, SparseCore 0:
  217.6 148.1 reduce-scatter.2
  472.2 39.2 reduce-scatter.4
where the time goes:
time: 537 us; the launch traced here: 536 us
  blocking collectives  445 us (83%)
  waiting for transfers between devices  38.7 us (7%)
  local copies, waits for them, and re-layouts  22.9 us (4%)
  between operations  15 us (3%)
  other arithmetic  9.58 us (2%)
    unnamed x1, blocking collectives  249 us
    pmax x1, blocking collectives, local(): all_top = lax.pmax(merged, 'req')  124 us
    all_gather x1, blocking collectives, local(): everyone = lax.all_gather(queries, 'req', axis=0, tiled=True)  56 us
    reduce_scatter x1, waiting for transfers between devices, local(): lax.psum_scatter(partial_value.astype(jnp.bfloat16), 'tp', scatter_dimens...  38.6 us
    psum x1, blocking collectives, local(): lax.psum((jnp.sum(hidden_mine, -1), jnp.sum(hidden_mine * hidden_mine, -1...  15.6 us
  transfers between devices with their start and end apart: 2, of which 1 were waited for; matrix products, arithmetic and copies ran while one was open for 1% of the time, Pallas kernels for 0%

commit v1 on v0

--- a/solution.py
+++ b/solution.py
@@ -43,7 +43,10 @@
     page_count = pool_cache.shape[0]
     tail_slots = tail_cache.shape[1]
     req_index = lax.axis_index("req")
-    everyone = lax.all_gather(queries, "req", axis=0, tiled=True)
+    y_new = lax.psum(1, axis_name="req")
+    z2 = jnp.stack([queries] * y_new)
+    then = lax.all_to_all(z2, "req", split_axis=0, concat_axis=0)
+    everyone = jnp.concatenate(then, axis=0)
     by_group = everyone.reshape(group_count, row_count, heads_here, HEAD)
     safe_group = jnp.clip(page_group, 0, group_count - 1)
     page_queries = by_group[safe_group]

time: 537 us -> 497 us (0.926)
  blocking collectives: 445 us -> 391 us
  starting transfers between devices: 0.08 us -> 13.9 us
    all_gather x1 -> x0, blocking collectives: 56 us -> none  [local(): everyone = lax.all_gather(queries, 'req', axis=0, tiled=True)]
    all_to_all x0 -> x1, starting transfers between devices: none -> 13.9 us  [local(): then = lax.all_to_all(z2, 'req', split_axis=0, concat_axis=0)]
  transfers between devices with their start and end apart: 2 -> 3, of which waited for: 1 -> 1; matrix products, arithmetic and copies ran while one was open for 1% -> 5% of each run, Pallas kernels for 0% -> 0%
where the time goes in v1:
time: 497 us
  blocking collectives  391 us (79%)
  waiting for transfers between devices  39.4 us (8%)
  local copies, waits for them, and re-layouts  25.4 us (5%)
  between operations  15 us (3%)
  starting transfers between devices  13.9 us (3%)
  other arithmetic  6.86 us (1%)
  matrix products  5.46 us (1%)
    unnamed x1, blocking collectives  249 us
    pmax x1, blocking collectives, local(): all_top = lax.pmax(merged, 'req')  126 us
    reduce_scatter x1, waiting for transfers between devices, local(): lax.psum_scatter(partial_value.astype(jnp.bfloat16), 'tp', scatter_dimens...  39.3 us
    psum x1, blocking collectives, local(): lax.psum((jnp.sum(hidden_mine, -1), jnp.sum(hidden_mine * hidden_mine, -1...  15.6 us
    all_to_all x1, starting transfers between devices, local(): then = lax.all_to_all(z2, 'req', split_axis=0, concat_axis=0)  13.9 us
    slice x1, local copies, waits for them, and re-layouts, local(): pool_cache[:, :, 1].reshape(page_count, PAGE, heads_here, HEAD)  11.7 us
  transfers between devices with their start and end apart: 3, of which 1 were waited for; matrix products, arithmetic and copies ran while one was open for 5% of the time, Pallas kernels for 0%

profile of v1, /device:TPU:2, one launch (start us, length us, event | category | flops | bytes accessed | tf_op | source)
XLA Modules:
  0.0 496.7 jit_solution(17686075630075350942)
XLA Ops:
  7.2 1.7 stack.2
  8.9 13.9 %all-to-all-start = ((bf16[64,16,256]{2,1,0:T(8,128)(2,1)}), bf16[64,16,256]{2,1,0:T(8,128)(2,1)S(1)}, u32[]{:S(2)}, u32[]{:S(2)}) async-start(bf16[64,16,256]{2,1,0:T(8,128)(2,1)} %stack.2), calls=%async_computation | async-start | bytes 1048576 | tf_op jit(solution)/shard_map/all_to_all | solution.py:48
  22.8 0.7 compare_select_fusion
  23.5 0.7 broadcast_compare_fusion
  24.1 0.7 iota_compare_fusion
  24.9 0.7 reshape.269
  25.6 0.7 reshape.224
  26.3 1.4 gather_fusion
  27.7 0.1 fusion.31
  27.8 2.8 slice_reduce_fusion.2
  30.9 0.2 fusion.17
  31.1 0.1 fusion.25
  31.2 0.1 fusion.46
  31.5 11.7 %slice_reduce_fusion = (bf16[32,64,256]{2,1,0:T(8,128)(2,1)S(1)}, bf16[32,64,256]{2,1,0:T(8,128)(2,1)}) fusion(bf16[32,64,2,256]{3,2,1,0:T(2,128)(2,1)} %param.17), kind=kLoop, calls=%fused_computation.5 | loop fusion | bytes 4194304 | tf_op jit(solution)/shard_map/slice | solution.py:54
  43.2 0.1 copy_bitcast_fusion
  43.3 0.6 gather_fusion.1
  43.9 2.0 fusion.48
  45.9 0.2 select_reduce_fusion
  46.1 0.1 copy.51
  46.2 0.1 reshape.223
  46.3 0.2 dynamic_update_slice.3
  46.5 125.9 %pmax.7 = f32[1024,2]{0,1:T(2,128)S(1)} all-reduce(f32[1024,2]{0,1:T(2,128)S(1)} %dynamic_update_slice.3), channel_id=1, replica_groups=mesh['req'=64,'tp'=8] {'req'}, use_global_device_ids=true, to_apply=%region_3.4 | all-reduce | flops 2048 | bytes 16384 | tf_op jit(solution)/shard_map/pmax | solution.py:91
  172.4 0.1 reshape.225
  172.5 0.6 gather_fusion.2
  173.2 0.4 fusion.11
  173.6 0.4 fusion.5
  174.0 0.5 fusion
  174.5 0.3 copy.55
  174.8 0.4 reshape.226
  175.2 0.4 fusion.35
  175.7 0.4 convolution_add_fusion
  176.1 1.1 reshape.227
  177.3 1.3 dynamic-slice
  179.5 0.3 fusion.38
  179.8 0.3 reshape.230
  180.1 249.1 %all-reduce = f32[1024,2]{1,0:T(8,128)S(1)} all-reduce(f32[1024,2]{1,0:T(8,128)S(1)} %reshape.230), channel_id=3, replica_groups=mesh['req'=64,'tp'=8] {'req'}, use_global_device_ids=true, to_apply=%region_6.7.clone | all-reduce | flops 2048 | bytes 16384
  429.3 0.2 fusion.36
  429.6 0.1 copy.56
  429.7 0.2 fusion.13
  429.9 0.2 fusion.15
  430.1 0.7 reshape.228
  430.9 0.1 fusion.32
  431.0 0.9 convolution_convert_fusion
  431.9 0.8 dynamic-slice_convert_fusion
  432.7 39.3 %reduce-scatter.5.cloned.1.call-done = bf16[16,256]{1,0:T(8,128)(2,1)} async-done(((bf16[16,2048]{1,0:T(8,128)(2,1)}), bf16[16,256]{1,0:T(8,128)(2,1)}) %reduce-scatter.5.cloned.1.call-update) | async-done | bytes 8208 | tf_op jit(solution)/shard_map/reduce_scatter | solution.py:129
  472.0 0.8 fusion.33
  472.8 15.6 %all-reduce.1 = (f32[16]{0:T(128)S(1)}, f32[16]{0:T(128)S(1)}) all-reduce(f32[16]{0:T(128)S(1)} %get-tuple-element.7, f32[16]{0:T(128)S(1)} %get-tuple-element.6), channel_id=1, replica_groups=mesh['req'=64,'tp'=8] {'tp'}, use_global_device_ids=true, to_apply=%region_12.13 | all-reduce | flops 32 | bytes 256 | tf_op jit(solution)/shard_map/psum | solution.py:136
  488.4 1.4 add_convert_fusion
  (50 shorter events, 1.3 us)
Async XLA Ops:
  7.2 423.8 %copy-start = (bf16[256,2048]{1,0:T(8,128)(2,1)S(1)}, bf16[256,2048]{1,0:T(8,128)(2,1)}, u32[]{:S(2)}) copy-start(bf16[256,2048]{1,0:T(8,128)(2,1)} %param.22) | copy-start | bytes 3145732
  7.2 20.5 %copy-start.6 = (s32[32]{0:T(128)S(1)}, s32[32]{0:T(128)}, u32[]{:S(2)}) copy-start(s32[32]{0:T(128)} %param.19) | copy-start | bytes 388
  7.2 20.6 %copy-start.1 = (bf16[16,32,2,256]{3,2,1,0:T(2,128)(2,1)S(1)}, bf16[16,32,2,256]{3,2,1,0:T(2,128)(2,1)}, u32[]{:S(2)}) copy-start(bf16[16,32,2,256]{3,2,1,0:T(2,128)(2,1)} %param.15) | copy-start | bytes 1572868
  7.2 23.5 %copy-start.7 = (s32[16]{0:T(128)S(1)}, s32[16]{0:T(128)}, u32[]{:S(2)}) copy-start(s32[16]{0:T(128)} %param.16) | copy-start | bytes 196
  7.2 23.5 %copy-start.3 = (bf16[16,2,256]{2,1,0:T(2,128)(2,1)S(1)}, bf16[16,2,256]{2,1,0:T(2,128)(2,1)}, u32[]{:S(2)}) copy-start(bf16[16,2,256]{2,1,0:T(2,128)(2,1)} %param.14) | copy-start | bytes 49156
  8.9 34.3 %all-to-all-start = ((bf16[64,16,256]{2,1,0:T(8,128)(2,1)}), bf16[64,16,256]{2,1,0:T(8,128)(2,1)S(1)}, u32[]{:S(2)}, u32[]{:S(2)}) async-start(bf16[64,16,256]{2,1,0:T(8,128)(2,1)} %stack.2), calls=%async_computation | async-start | bytes 1048576 | tf_op jit(solution)/shard_map/all_to_all | solution.py:48
  22.8 407.4 %reduce-scatter.3.cloned.1.call-start = ((), (), s32[]{:S(2)}) async-start(), calls=%async_computation.3 | async-start | bytes 1064960 | tf_op jit(solution)/shard_map/reduce_scatter | solution.py:111
  174.5 0.8 copy-start.5
  176.1 253.7 %copy-start.2 = (bf16[16,32,256]{2,1,0:T(8,128)(2,1)S(1)}, bf16[16,32,256]{2,1,0:T(8,128)(2,1)}, u32[]{:S(2)}) copy-start(bf16[16,32,256]{2,1,0:T(8,128)(2,1)} %get-tuple-element.4) | copy-start | bytes 786436
  177.3 254.6 %copy-start.8 = (bf16[256]{0:T(256)(128)(2,1)S(1)}, bf16[256]{0:T(256)(128)(2,1)}, u32[]{:S(2)}) copy-start(bf16[256]{0:T(256)(128)(2,1)} %param.24) | copy-start | bytes 1540
  177.3 254.6 %copy-start.9 = (bf16[256]{0:T(256)(128)(2,1)S(1)}, bf16[256]{0:T(256)(128)(2,1)}, u32[]{:S(2)}) copy-start(bf16[256]{0:T(256)(128)(2,1)} %param.25) | copy-start | bytes 1540
  177.3 294.7 %reduce-scatter.5.cloned.1.call-start = ((), (), s32[]{:S(2)}) async-start(), calls=%async_computation.4 | async-start | bytes 73728 | tf_op jit(solution)/shard_map/reduce_scatter | solution.py:129
  472.8 17.0 %copy-start.4 = (bf16[16,256]{1,0:T(8,128)(2,1)}, bf16[16,256]{1,0:T(8,128)(2,1)S(1)}, u32[]{:S(2)}) copy-start(bf16[16,256]{1,0:T(8,128)(2,1)S(1)} %get-tuple-element.10) | copy-start | bytes 24580
Sparse Core Ops, SparseCore 0:
  177.4 148.7 reduce-scatter.2
  432.0 39.9 reduce-scatter.4
